TPU v7x, 256 devices: a whole 4x4x8 slice. The times are simulated.
256 devices in a mesh: sub: 16 (over z, core), fr: 16 (over y, x).
Axes of the slice: x: 4, y: 4, z: 8, core: 2. Of those that a mesh axis runs over, the one named last changes fastest.
Arguments:
- front_leaf: bfloat16 [32768, 2048], P(('sub', 'fr')), as said below
- shares_one: float32 [32768, 384], P(('sub', 'fr')), as said below
- shares_two: float32 [32768, 384], P(('sub', 'fr')), as said below
- map_leaf: int32 [16, 13], P('sub'), may hold values from 0 to 15, as said below
- map_mid: int32 [8, 13], replicated, may hold values from 0 to 15, as said below
Outputs:
- leaf_panel: float32 [32768, 384], P(('sub', 'fr'))
- middle_panel: float32 [32768, 384], P(('sub', 'fr'))
- top_panel: float32 [32768, 384], P(('sub', 'fr'))
- contribution: float32 [32768, 1664], P(('sub', 'fr'))
Inputs may be any that keep to these rules, and one draw needn't show every extreme that they name: `front_leaf`: each block of 2048 rows is a symmetric positive definite front. `shares_one`: in each block of 2048 rows the first 384 rows are symmetric; with the extended contributions every middle front is positive definite. `shares_two`: in each block of 2048 rows the first 384 rows are symmetric; with the extended contributions every top front is positive definite. `map_leaf`: each row lists 13 different blocks; rows 2q and 2q+1 together name every block of their parent. `map_mid`: each row lists 13 different blocks; rows 2r and 2r+1 together name every block of their parent.
All inputs are finite; a program needn't handle non-finite values.
Results may differ from a plain program's by a relative error of at most 0.0003.
Values sent between devices are 32-bit elements; how exact they have to be, the bound alone decides.
No kernel may reach another device: no remote copies, remote signals or barrier semaphores. Data moves between devices by JAX's collectives and lax.ppermute only.
A program may use at most 128 MiB of HBM per device.

v0:
```python
import jax
import jax.numpy as jnp
from jax import lax
from jax.sharding import PartitionSpec as P

BLK = 128
P_SIZE = 384
NFB = 16
NPB = 3
HIGH = lax.Precision.HIGHEST


def partner(array, axis, stride):
    return lax.ppermute(array, axis, [(i, i ^ 1 << stride) for i in range(lax.axis_size(axis))])


def eliminate(front, row_start):
    row_count, front_order = front.shape
    panels = []
    for block_index in range(NPB):
        block_low = block_index * BLK
        gathered = lax.all_gather(front[:, block_low : block_low + BLK], "fr", axis=0, tiled=True)
        row_ids = jnp.arange(front_order)
        lower_block = jnp.linalg.cholesky(gathered[block_low : block_low + BLK])
        solved = lax.linalg.triangular_solve(
            lower_block, gathered, left_side=False, lower=True, transpose_a=True
        )
        below = jnp.where((row_ids >= block_low + BLK)[:, None], solved, 0.0)
        placed = below.at[block_low : block_low + BLK].set(lower_block)
        own_below = lax.dynamic_slice_in_dim(below, row_start, row_count, 0)
        own_panel = lax.dynamic_slice_in_dim(placed, row_start, row_count, 0)
        front = front - jnp.dot(
            own_below, below.T, precision=HIGH, preferred_element_type=jnp.float32
        )
        panels.append(own_panel)
    return (jnp.concatenate(panels, axis=1), front)


def make_table(block_map):
    padded = jnp.concatenate([jnp.full((NPB,), -1, jnp.int32), block_map])
    return (padded[:, None] == jnp.arange(NFB, dtype=jnp.int32)[None, :]).astype(jnp.float32)


def extend(front, block_map, row_start):
    row_count, front_order = front.shape
    block_share = row_count // BLK
    block_table = make_table(block_map)
    padded = jnp.concatenate([jnp.full((NPB,), -1, jnp.int32), block_map])
    parents = row_start // BLK + jnp.arange(block_share)
    matches = padded[None, :] == parents[:, None]
    present = jnp.any(matches, axis=1)
    source_block = jnp.sum(jnp.where(matches, jnp.arange(NFB)[None, :], 0), axis=1)
    source_rows = (source_block[:, None] * BLK + jnp.arange(BLK)[None, :]).reshape(row_count)
    is_live = jnp.repeat(present, BLK)
    shard_rows = lax.all_gather(front, "fr", axis=0, tiled=True)
    inside = is_live & (source_rows >= 0) & (source_rows < shard_rows.shape[0])
    picked_rows = jnp.take(shard_rows, jnp.clip(source_rows, 0, shard_rows.shape[0] - 1), axis=0)
    picked_rows = jnp.where(inside[:, None], picked_rows, 0.0)
    mapped = jnp.einsum(
        "rqc,qe->rec", picked_rows.reshape(row_count, NFB, BLK), block_table, precision=HIGH
    )
    return mapped.reshape(row_count, front_order)


def combine(front, shares, block_map, row_start, level_bit):
    front_order = front.shape[1]
    piece_part = extend(front, block_map, row_start) + jnp.pad(
        shares, ((0, 0), (0, front_order - P_SIZE))
    )
    return piece_part + partner(piece_part, "sub", level_bit)


def local(front_leaf, shares_one, shares_two, map_leaf, map_mid):
    row_count = front_leaf.shape[0]
    row_start = lax.axis_index("fr") * row_count
    sub_index = lax.axis_index("sub")
    leaf_panel, child_front = eliminate(front_leaf.astype(jnp.float32), row_start)
    shares_sum = shares_two + partner(shares_two, "sub", 0)
    middle_front = combine(child_front, shares_one, map_leaf[0], row_start, 0)
    middle_panel, middle_front = eliminate(middle_front, row_start)
    pair_map = lax.dynamic_index_in_dim(map_mid, sub_index // 2, 0, keepdims=False)
    top_front = combine(middle_front, shares_sum, pair_map, row_start, 1)
    top_panel, top_front = eliminate(top_front, row_start)
    row_ids = row_start + jnp.arange(row_count)
    contribution = jnp.where((row_ids >= P_SIZE)[:, None], top_front[:, P_SIZE:], 0.0)
    return (leaf_panel, middle_panel, top_panel, contribution)


def solution(mesh):
    in_specs = (
        P(("sub", "fr"), None),
        P(("sub", "fr"), None),
        P(("sub", "fr"), None),
        P("sub", None),
        P(),
    )
    out_specs = (
        P(("sub", "fr"), None),
        P(("sub", "fr"), None),
        P(("sub", "fr"), None),
        P(("sub", "fr"), None),
    )
    return jax.shard_map(local, mesh=mesh, in_specs=in_specs, out_specs=out_specs, check_vma=False)
```

profile of v0, /device:TPU:2, one launch (start us, length us, event | category | flops | bytes accessed | tf_op | source)
XLA Modules:
  0.0 1077.1 jit_solution(2914424873114445792)
XLA Ops:
  9.3 52.5 %all-gather.12.cloned.1.call-done = f32[2048,128]{0,1:T(8,128)} async-done(((f32[128,128]{0,1:T(8,128)}), f32[2048,128]{0,1:T(8,128)}) %all-gather.12.cloned.1.call-update) | async-done | bytes 1048592 | tf_op jit(solution)/shard_map/all_gather | solution.py:22
  63.6 11.7 %cholesky.149 = f32[128,128]{1,0:T(8,128)S(1)} custom-call(f32[128,128]{1,0:T(8,128)S(1)} %fusion.29), custom_call_target="Cholesky" | custom-call | tf_op jit(solution)/shard_map/jit(cholesky)/cholesky | solution.py:24
  76.6 9.8 custom-call.13
  86.5 2.3 fusion.8
  88.7 1.8 convolution_subtract_fusion.7
  91.5 47.4 %all-gather.14.cloned.1.call-done = f32[2048,128]{0,1:T(8,128)} async-done(((f32[128,128]{0,1:T(8,128)}), f32[2048,128]{0,1:T(8,128)}) %all-gather.14.cloned.1.call-update) | async-done | bytes 1048592 | tf_op jit(solution)/shard_map/all_gather | solution.py:22
  140.7 11.7 %cholesky.160 = f32[128,128]{1,0:T(8,128)S(1)} custom-call(f32[128,128]{1,0:T(8,128)S(1)} %fusion.27), custom_call_target="Cholesky" | custom-call | tf_op jit(solution)/shard_map/jit(cholesky)/cholesky | solution.py:24
  153.8 9.8 custom-call.14
  163.6 2.3 fusion.7
  165.8 1.8 convolution_subtract_fusion.6
  169.8 47.2 %all-gather.16.cloned.1.call-done = f32[2048,128]{0,1:T(8,128)} async-done(((f32[128,128]{0,1:T(8,128)}), f32[2048,128]{0,1:T(8,128)}) %all-gather.16.cloned.1.call-update) | async-done | bytes 1048592 | tf_op jit(solution)/shard_map/all_gather | solution.py:22
  218.8 11.7 %cholesky.171 = f32[128,128]{1,0:T(8,128)S(1)} custom-call(f32[128,128]{1,0:T(8,128)S(1)} %fusion.25), custom_call_target="Cholesky" | custom-call | tf_op jit(solution)/shard_map/jit(cholesky)/cholesky | solution.py:24
  231.9 9.8 custom-call.15
  241.7 2.3 fusion.6
  244.9 4.0 convolution_subtract_fusion.5
  252.2 1.4 compare_reduce_fusion.10
  255.3 118.1 %all-gather.18.cloned.1.call-done = f32[2048,2048]{0,1:T(8,128)} async-done(((f32[128,2048]{0,1:T(8,128)}), f32[2048,2048]{0,1:T(8,128)}) %all-gather.18.cloned.1.call-update) | async-done | bytes 16777232 | tf_op jit(solution)/shard_map/all_gather | solution.py:55
  373.4 17.6 %copy.19 = f32[2048,2048]{1,0:T(8,128)} copy(f32[2048,2048]{0,1:T(8,128)} %all-gather.18.cloned.1.call-done) | data formatting | bytes 33554432 | tf_op jit(solution)/shard_map/all_gather | solution.py:55
  391.0 7.3 gather_fusion
  400.7 1.4 copy.20
  402.1 1.3 bitcast_add_fusion.1
  403.6 2.6 collective-permute-done
  407.0 47.7 %all-gather.20.cloned.1.call-done = f32[2048,128]{0,1:T(8,128)} async-done(((f32[128,128]{0,1:T(8,128)}), f32[2048,128]{0,1:T(8,128)}) %all-gather.20.cloned.1.call-update) | async-done | bytes 1048592 | tf_op jit(solution)/shard_map/all_gather | solution.py:22
  456.5 11.7 %cholesky.182 = f32[128,128]{1,0:T(8,128)S(1)} custom-call(f32[128,128]{1,0:T(8,128)S(1)} %fusion.23), custom_call_target="Cholesky" | custom-call | tf_op jit(solution)/shard_map/jit(cholesky)/cholesky | solution.py:24
  470.2 9.8 custom-call.16
  480.0 2.3 fusion.5
  482.3 1.8 convolution_subtract_fusion.4
  486.0 47.4 %all-gather.22.cloned.1.call-done = f32[2048,128]{0,1:T(8,128)} async-done(((f32[128,128]{0,1:T(8,128)}), f32[2048,128]{0,1:T(8,128)}) %all-gather.22.cloned.1.call-update) | async-done | bytes 1048592 | tf_op jit(solution)/shard_map/all_gather | solution.py:22
  535.2 11.7 %cholesky.193 = f32[128,128]{1,0:T(8,128)S(1)} custom-call(f32[128,128]{1,0:T(8,128)S(1)} %fusion.21), custom_call_target="Cholesky" | custom-call | tf_op jit(solution)/shard_map/jit(cholesky)/cholesky | solution.py:24
  548.9 9.8 custom-call.17
  558.7 2.3 fusion.4
  562.0 3.0 convolution_subtract_fusion.3
  566.1 47.2 %all-gather.24.cloned.1.call-done = f32[2048,128]{0,1:T(8,128)} async-done(((f32[128,128]{0,1:T(8,128)}), f32[2048,128]{0,1:T(8,128)}) %all-gather.24.cloned.1.call-update) | async-done | bytes 1048592 | tf_op jit(solution)/shard_map/all_gather | solution.py:22
  615.2 11.7 %cholesky.204 = f32[128,128]{1,0:T(8,128)S(1)} custom-call(f32[128,128]{1,0:T(8,128)S(1)} %fusion.19), custom_call_target="Cholesky" | custom-call | tf_op jit(solution)/shard_map/jit(cholesky)/cholesky | solution.py:24
  628.8 9.8 custom-call.18
  638.7 2.3 fusion.3
  641.9 2.8 convolution_subtract_fusion.2
  650.6 118.5 %all-gather.26.cloned.1.call-done = f32[2048,2048]{0,1:T(8,128)} async-done(((f32[128,2048]{0,1:T(8,128)}), f32[2048,2048]{0,1:T(8,128)}) %all-gather.26.cloned.1.call-update) | async-done | bytes 16777232 | tf_op jit(solution)/shard_map/all_gather | solution.py:55
  769.2 17.6 %copy.31 = f32[2048,2048]{1,0:T(8,128)} copy(f32[2048,2048]{0,1:T(8,128)} %all-gather.26.cloned.1.call-done) | data formatting | bytes 33554432 | tf_op jit(solution)/shard_map/all_gather | solution.py:55
  786.8 7.3 gather_fusion.1
  796.5 1.4 copy.32
  797.9 1.3 bitcast_add_fusion
  799.3 1.6 collective-permute-start.2
  800.9 22.0 %collective-permute-done.2 = f32[128,2048]{0,1:T(8,128)S(1)} collective-permute-done((f32[128,2048]{0,1:T(8,128)S(1)}, f32[128,2048]{0,1:T(8,128)S(1)}, u32[]{:S(2)}, u32[]{:S(2)}) %collective-permute-start.2) | collective-permute-done | bytes 1048608 | tf_op jit(solution)/shard_map/ppermute | solution.py:14
  823.7 47.7 %all-gather.28.cloned.1.call-done = f32[2048,128]{0,1:T(8,128)} async-done(((f32[128,128]{0,1:T(8,128)}), f32[2048,128]{0,1:T(8,128)}) %all-gather.28.cloned.1.call-update) | async-done | bytes 1048592 | tf_op jit(solution)/shard_map/all_gather | solution.py:22
  871.4 1.5 slice.252
  872.9 1.6 copy.35
  874.4 1.5 fusion.17
  875.9 13.2 %cholesky.215 = f32[128,128]{1,0:T(8,128)} custom-call(f32[128,128]{1,0:T(8,128)} %fusion.17), custom_call_target="Cholesky" | custom-call | tf_op jit(solution)/shard_map/jit(cholesky)/cholesky | solution.py:24
  890.6 2.2 select_bitcast_fusion.2
  892.8 11.3 %custom-call.19 = f32[1,128,128]{1,2,0:T(8,128)} custom-call(f32[1,128,128]{2,1,0:T(8,128)} %get-tuple-element.123), custom_call_target="InvertDiagBlocksLowerTriangular" | custom-call | tf_op jit(solution)/shard_map/triangular_solve/custom-call.0 | solution.py:25
  904.1 2.3 fusion.2
  906.4 1.8 convolution_subtract_fusion.1
  910.9 46.7 %all-gather.30.cloned.1.call-done = f32[2048,128]{0,1:T(8,128)} async-done(((f32[128,128]{0,1:T(8,128)}), f32[2048,128]{0,1:T(8,128)}) %all-gather.30.cloned.1.call-update) | async-done | bytes 1048592 | tf_op jit(solution)/shard_map/all_gather | solution.py:22
  959.4 11.7 %cholesky.226 = f32[128,128]{1,0:T(8,128)S(1)} custom-call(f32[128,128]{1,0:T(8,128)S(1)} %fusion.15), custom_call_target="Cholesky" | custom-call | tf_op jit(solution)/shard_map/jit(cholesky)/cholesky | solution.py:24
  972.5 10.4 custom-call.20
  982.9 2.3 fusion.1
  985.2 3.0 convolution_subtract_fusion
  1003.0 34.7 %all-gather.32.cloned.1.call-done = f32[2048,128]{0,1:T(8,128)} async-done(((f32[128,128]{0,1:T(8,128)}), f32[2048,128]{0,1:T(8,128)}) %all-gather.32.cloned.1.call-update) | async-done | bytes 1048592 | tf_op jit(solution)/shard_map/all_gather | solution.py:22
  1039.4 11.9 %cholesky.237 = f32[128,128]{1,0:T(8,128)S(1)} custom-call(f32[128,128]{1,0:T(8,128)S(1)} %fusion.13), custom_call_target="Cholesky" | custom-call | tf_op jit(solution)/shard_map/jit(cholesky)/cholesky | solution.py:24
  1052.7 9.8 custom-call.21
  1062.5 2.3 fusion
  1064.8 1.8 fusion.31
  1067.6 1.3 fusion.11
  (172 shorter events, 74.6 us)
Async XLA Ops:
  7.2 639.0 %copy-start = (s32[8,13]{1,0:T(8,128)S(1)}, s32[8,13]{1,0:T(8,128)}, u32[]{:S(2)}) copy-start(s32[8,13]{1,0:T(8,128)} %param.32) | copy-start | bytes 1252
  7.2 242.1 %copy-start.13 = (s32[1,13]{1,0:T(1,128)S(1)}, s32[1,13]{1,0:T(1,128)}, u32[]{:S(2)}) copy-start(s32[1,13]{1,0:T(1,128)} %param.31) | copy-start | bytes 160
  7.2 54.6 %all-gather.12.cloned.1.call-start = ((), (), s32[]{:S(2)}) async-start(), calls=%async_computation | async-start | bytes 1114112 | tf_op jit(solution)/shard_map/all_gather | solution.py:22
  9.2 129.7 %all-gather.14.cloned.1.call-start = ((), (), s32[]{:S(2)}) async-start(), calls=%async_computation.1 | async-start | bytes 1114112 | tf_op jit(solution)/shard_map/all_gather | solution.py:22
  91.2 125.8 %all-gather.16.cloned.1.call-start = ((), (), s32[]{:S(2)}) async-start(), calls=%async_computation.2 | async-start | bytes 1114112 | tf_op jit(solution)/shard_map/all_gather | solution.py:22
  167.7 1.0 copy-start.7
  169.3 204.1 %all-gather.18.cloned.1.call-start = ((), (), s32[]{:S(2)}) async-start(), calls=%async_computation.3 | async-start | bytes 17825792 | tf_op jit(solution)/shard_map/all_gather | solution.py:55
  243.9 1.0 copy-start.1
  249.0 205.7 %all-gather.20.cloned.1.call-start = ((), (), s32[]{:S(2)}) async-start(), calls=%async_computation.4 | async-start | bytes 1114112 | tf_op jit(solution)/shard_map/all_gather | solution.py:22
  403.5 2.7 collective-permute-start
  407.0 126.4 %all-gather.22.cloned.1.call-start = ((), (), s32[]{:S(2)}) async-start(), calls=%async_computation.5 | async-start | bytes 1114112 | tf_op jit(solution)/shard_map/all_gather | solution.py:22
  482.2 1.8 copy-start.2
  484.1 1.0 copy-start.8
  485.7 127.6 %all-gather.24.cloned.1.call-start = ((), (), s32[]{:S(2)}) async-start(), calls=%async_computation.6 | async-start | bytes 1114112 | tf_op jit(solution)/shard_map/all_gather | solution.py:22
  561.0 1.0 copy-start.3
  565.7 203.5 %all-gather.26.cloned.1.call-start = ((), (), s32[]{:S(2)}) async-start(), calls=%async_computation.7 | async-start | bytes 17825792 | tf_op jit(solution)/shard_map/all_gather | solution.py:55
  640.9 1.0 copy-start.4
  644.8 226.6 %all-gather.28.cloned.1.call-start = ((), (), s32[]{:S(2)}) async-start(), calls=%async_computation.8 | async-start | bytes 1114112 | tf_op jit(solution)/shard_map/all_gather | solution.py:22
  645.9 4.7 collective-permute-start.1
  799.2 195.6 %copy-start.10 = (f32[128,128]{1,0:T(8,128)S(1)}, f32[128,128]{1,0:T(8,128)}, u32[]{:S(2)}) copy-start(f32[128,128]{1,0:T(8,128)} %get-tuple-element.130) | copy-start | bytes 196612
  799.3 197.1 %copy-start.11 = (f32[128,128]{1,0:T(8,128)S(1)}, f32[128,128]{1,0:T(8,128)}, u32[]{:S(2)}) copy-start(f32[128,128]{1,0:T(8,128)} %get-tuple-element.128) | copy-start | bytes 196612
  799.3 198.7 %copy-start.12 = (f32[128,128]{1,0:T(8,128)S(1)}, f32[128,128]{1,0:T(8,128)}, u32[]{:S(2)}) copy-start(f32[128,128]{1,0:T(8,128)} %get-tuple-element.126) | copy-start | bytes 196612
  799.3 23.6 %collective-permute-start.2 = (f32[128,2048]{0,1:T(8,128)S(1)}, f32[128,2048]{0,1:T(8,128)S(1)}, u32[]{:S(2)}, u32[]{:S(2)}) collective-permute-start(f32[128,2048]{0,1:T(8,128)S(1)} %bitcast_add_fusion), channel_id=1, source_target_pairs={{0,32},{16,48},{32,0},{48,16},{64,96},{80,112},{96,64},{112,80},{1... | collective-permute-start | bytes 3145736 | tf_op jit(solution)/shard_map/ppermute | solution.py:14
  823.7 133.9 %all-gather.30.cloned.1.call-start = ((), (), s32[]{:S(2)}) async-start(), calls=%async_computation.9 | async-start | bytes 1114112 | tf_op jit(solution)/shard_map/all_gather | solution.py:22
  906.4 1.8 copy-start.5
  908.2 1.0 copy-start.6
  909.9 127.7 %all-gather.32.cloned.1.call-start = ((), (), s32[]{:S(2)}) async-start(), calls=%async_computation.10 | async-start | bytes 1114112 | tf_op jit(solution)/shard_map/all_gather | solution.py:22
  988.2 1.0 copy-start.9
Sparse Core Ops, SparseCore 0:
  11.0 50.7 all-gather.11
  91.3 47.5 all-gather.13
  169.4 47.5 all-gather.15
  249.1 124.2 all-gather.17
  407.1 47.5 all-gather.19
  485.9 47.5 all-gather.21
  565.8 47.5 all-gather.23
  644.9 124.2 all-gather.25
  823.8 47.5 all-gather.27
  910.0 47.5 all-gather.29
  990.1 47.5 all-gather.31
where the time goes:
time: 1090 us; the launch traced here: 1080 us
  waiting for transfers between devices  680 us (62%)
  other arithmetic  237 us (22%)
  local copies, waits for them, and re-layouts  94.7 us (9%)
  matrix products  44.9 us (4%)
  between operations  16.4 us (2%)
    all_gather x9, waiting for transfers between devices, eliminate(): lax.all_gather(front[:, block_low:block_low + BLK], 'fr', axis=0, tiled=T...  419 us
    all_gather x2, waiting for transfers between devices, extend(): shard_rows = lax.all_gather(front, 'fr', axis=0, tiled=True)  237 us
    another operation x27, other arithmetic, eliminate(): lower_block = jnp.linalg.cholesky(gathered[block_low:block_low + BLK])  114 us
    another operation x18, other arithmetic, eliminate(): lax.linalg.triangular_solve(lower_block, gathered, left_side=False, lower...  99.7 us
    all_gather x2, local copies, waits for them, and re-layouts, extend(): shard_rows = lax.all_gather(front, 'fr', axis=0, tiled=True)  35.2 us
    ppermute x3, waiting for transfers between devices, partner(): lax.ppermute(array, axis, [(i, i ^ 1 << stride) for i in range(lax.axis_s...  24.6 us
    dot_general x9, matrix products, eliminate(): jnp.dot(own_below, below.T, precision=HIGH, preferred_element_type=jnp.fl...  22 us
  transfers between devices with their start and end apart: 14, of which 13 were waited for; matrix products, arithmetic and copies ran while one was open for 2% of the time, Pallas kernels for 0%

commit v1 on v0

--- a/solution.py
+++ b/solution.py
@@ -19,7 +19,16 @@
     panels = []
     for block_index in range(NPB):
         block_low = block_index * BLK
-        gathered = lax.all_gather(front[:, block_low : block_low + BLK], "fr", axis=0, tiled=True)
+        x0 = front[:, block_low : block_low + BLK]
+        gathered = jnp.concatenate(
+            lax.all_to_all(
+                jnp.stack(lax.psum(1, axis_name="fr") * [x0]),
+                axis_name="fr",
+                split_axis=0,
+                concat_axis=0,
+            ),
+            axis=0,
+        )
         row_ids = jnp.arange(front_order)
         lower_block = jnp.linalg.cholesky(gathered[block_low : block_low + BLK])
         solved = lax.linalg.triangular_solve(

time: 1090 us -> 761 us (0.70)
  waiting for transfers between devices: 680 us -> 308 us
  blocking collectives: 0 us -> 81.3 us
  local copies, waits for them, and re-layouts: 94.7 us -> 53.1 us
  starting transfers between devices: 4.07 us -> 31 us
  matrix products: 44.9 us -> 33 us
    all_gather x9 -> x0, waiting for transfers between devices: 419 us -> none  [eliminate(): lax.all_gather(front[:, block_low:block_low + BLK], 'fr', axis=0, tiled=T...]
    all_to_all x0 -> x4, blocking collectives: none -> 81.3 us  [eliminate(): lax.all_to_all(jnp.stack(lax.psum(1, axis_name='fr') * [x0]), axis_name='...]
    all_to_all x0 -> x5, waiting for transfers between devices: none -> 58.8 us  [eliminate(): lax.all_to_all(jnp.stack(lax.psum(1, axis_name='fr') * [x0]), axis_name='...]
    all_gather x2 -> x0, local copies, waits for them, and re-layouts: 35.2 us -> none  [extend(): shard_rows = lax.all_gather(front, 'fr', axis=0, tiled=True)]
    all_to_all x0 -> x5, starting transfers between devices: none -> 28.5 us  [eliminate(): lax.all_to_all(jnp.stack(lax.psum(1, axis_name='fr') * [x0]), axis_name='...]
    all_gather x2, waiting for transfers between devices: 237 us -> 223 us  [extend(): shard_rows = lax.all_gather(front, 'fr', axis=0, tiled=True)]
  transfers between devices with their start and end apart: 14 -> 10, of which waited for: 13 -> 9; matrix products, arithmetic and copies ran while one was open for 2% -> 3% of each run, Pallas kernels for 0% -> 0%
where the time goes in v1:
time: 761 us; the launch traced here: 751 us
  waiting for transfers between devices  308 us (40%)
  other arithmetic  229 us (30%)
  blocking collectives  81.3 us (11%)
  local copies, waits for them, and re-layouts  53.1 us (7%)
  matrix products  33 us (4%)
  starting transfers between devices  31 us (4%)
  between operations  16.8 us (2%)
    all_gather x2, waiting for transfers between devices, extend(): shard_rows = lax.all_gather(front, 'fr', axis=0, tiled=True)  223 us
    another operation x27, other arithmetic, eliminate(): lower_block = jnp.linalg.cholesky(gathered[block_low:block_low + BLK])  114 us
    another operation x18, other arithmetic, eliminate(): lax.linalg.triangular_solve(lower_block, gathered, left_side=False, lower...  101 us
    all_to_all x4, blocking collectives, eliminate(): lax.all_to_all(jnp.stack(lax.psum(1, axis_name='fr') * [x0]), axis_name='...  81.3 us
    all_to_all x5, waiting for transfers between devices, eliminate(): lax.all_to_all(jnp.stack(lax.psum(1, axis_name='fr') * [x0]), axis_name='...  58.8 us
    all_to_all x5, starting transfers between devices, eliminate(): lax.all_to_all(jnp.stack(lax.psum(1, axis_name='fr') * [x0]), axis_name='...  28.5 us
    ppermute x3, waiting for transfers between devices, partner(): lax.ppermute(array, axis, [(i, i ^ 1 << stride) for i in range(lax.axis_s...  25.8 us
    dot_general x9, matrix products, eliminate(): jnp.dot(own_below, below.T, precision=HIGH, preferred_element_type=jnp.fl...  16.3 us
  transfers between devices with their start and end apart: 10, of which 9 were waited for; matrix products, arithmetic and copies ran while one was open for 3% of the time, Pallas kernels for 0%

profile of v1, /device:TPU:2, one launch (start us, length us, event | category | flops | bytes accessed | tf_op | source)
XLA Modules:
  0.0 751.5 jit_solution(5482227822007001319)
XLA Ops:
  9.1 7.5 all-to-all-start
  16.6 15.8 %all-to-all-done = f32[16,128,128]{1,2,0:T(8,128)S(1)} async-done(((f32[16,128,128]{1,2,0:T(8,128)}), f32[16,128,128]{1,2,0:T(8,128)S(1)}, u32[]{:S(2)}, u32[]{:S(2)}) %all-to-all-start) | async-done | bytes 1048608 | tf_op jit(solution)/shard_map/all_to_all | solution.py:24
  32.5 11.7 %cholesky.149 = f32[128,128]{1,0:T(8,128)S(1)} custom-call(f32[128,128]{1,0:T(8,128)S(1)} %fusion.20), custom_call_target="Cholesky" | custom-call | tf_op jit(solution)/shard_map/jit(cholesky)/cholesky | solution.py:33
  45.6 9.8 %custom-call.13 = f32[1,128,128]{1,2,0:T(8,128)S(1)} custom-call(f32[1,128,128]{2,1,0:T(8,128)S(1)} %get-tuple-element.139), custom_call_target="InvertDiagBlocksLowerTriangular" | custom-call | tf_op jit(solution)/shard_map/triangular_solve/custom-call.0 | solution.py:34
  56.8 2.1 convolution_subtract_fusion.7
  60.1 1.1 stack.19
  61.2 5.7 all-to-all-start.1
  66.9 15.0 %all-to-all-done.1 = f32[16,128,128]{1,2,0:T(8,128)S(1)} async-done(((f32[16,128,128]{1,2,0:T(8,128)}), f32[16,128,128]{1,2,0:T(8,128)S(1)}, u32[]{:S(2)}, u32[]{:S(2)}) %all-to-all-start.1) | async-done | bytes 1048608 | tf_op jit(solution)/shard_map/all_to_all | solution.py:24
  82.1 11.7 %cholesky.160 = f32[128,128]{1,0:T(8,128)S(1)} custom-call(f32[128,128]{1,0:T(8,128)S(1)} %fusion.19), custom_call_target="Cholesky" | custom-call | tf_op jit(solution)/shard_map/jit(cholesky)/cholesky | solution.py:33
  95.1 9.8 %custom-call.14 = f32[1,128,128]{1,2,0:T(8,128)S(1)} custom-call(f32[1,128,128]{2,1,0:T(8,128)S(1)} %get-tuple-element.137), custom_call_target="InvertDiagBlocksLowerTriangular" | custom-call | tf_op jit(solution)/shard_map/triangular_solve/custom-call.0 | solution.py:34
  107.4 2.3 convolution_subtract_fusion.6
  110.9 4.8 all-to-all-start.2
  116.2 14.7 %all-to-all-done.2 = f32[16,128,128]{1,2,0:T(8,128)S(1)} async-done(((f32[16,128,128]{1,2,0:T(8,128)}), f32[16,128,128]{1,2,0:T(8,128)S(1)}, u32[]{:S(2)}, u32[]{:S(2)}) %all-to-all-start.2) | async-done | bytes 1048608 | tf_op jit(solution)/shard_map/all_to_all | solution.py:24
  131.0 11.7 %cholesky.171 = f32[128,128]{1,0:T(8,128)S(1)} custom-call(f32[128,128]{1,0:T(8,128)S(1)} %fusion.18), custom_call_target="Cholesky" | custom-call | tf_op jit(solution)/shard_map/jit(cholesky)/cholesky | solution.py:33
  143.4 1.3 select_bitcast_fusion.6
  144.7 11.3 %custom-call.15 = f32[1,128,128]{1,2,0:T(8,128)} custom-call(f32[1,128,128]{2,1,0:T(8,128)} %get-tuple-element.135), custom_call_target="InvertDiagBlocksLowerTriangular" | custom-call | tf_op jit(solution)/shard_map/triangular_solve/custom-call.0 | solution.py:34
  156.0 1.3 copy.49
  157.3 2.3 fusion.6
  160.6 2.1 convolution_subtract_fusion.5
  162.8 1.4 fusion.63
  164.8 1.4 compare_reduce_fusion.10
  166.9 112.2 %all-gather.3.cloned.1.call-done = f32[2048,2048]{1,0:T(8,128)} async-done(((f32[128,2048]{1,0:T(8,128)}), f32[2048,2048]{1,0:T(8,128)}) %all-gather.3.cloned.1.call-update) | async-done | bytes 16777232 | tf_op jit(solution)/shard_map/all_gather | solution.py:64
  279.0 7.2 gather_fusion
  287.8 2.6 collective-permute-done
  290.8 21.6 %all_to_all.45 = f32[16,128,128]{1,2,0:T(8,128)S(1)} all-to-all(f32[16,128,128]{1,2,0:T(8,128)S(1)} %stack.21), channel_id=1, replica_groups=mesh['sub'=16,'fr'=16] {'fr'}, dimensions={0} | all-to-all | bytes 2097152 | tf_op jit(solution)/shard_map/all_to_all | solution.py:24
  312.5 11.7 %cholesky.182 = f32[128,128]{1,0:T(8,128)S(1)} custom-call(f32[128,128]{1,0:T(8,128)S(1)} %fusion.17), custom_call_target="Cholesky" | custom-call | tf_op jit(solution)/shard_map/jit(cholesky)/cholesky | solution.py:33
  325.5 9.8 %custom-call.16 = f32[1,128,128]{1,2,0:T(8,128)S(1)} custom-call(f32[1,128,128]{2,1,0:T(8,128)S(1)} %get-tuple-element.133), custom_call_target="InvertDiagBlocksLowerTriangular" | custom-call | tf_op jit(solution)/shard_map/triangular_solve/custom-call.0 | solution.py:34
  335.4 1.4 copy.53
  336.7 2.3 fusion.5
  340.3 19.8 %all_to_all.46 = f32[16,128,128]{1,2,0:T(8,128)S(1)} all-to-all(f32[16,128,128]{1,2,0:T(8,128)S(1)} %stack.22), channel_id=1, replica_groups=mesh['sub'=16,'fr'=16] {'fr'}, dimensions={0} | all-to-all | bytes 2097152 | tf_op jit(solution)/shard_map/all_to_all | solution.py:24
  360.3 11.7 %cholesky.193 = f32[128,128]{1,0:T(8,128)S(1)} custom-call(f32[128,128]{1,0:T(8,128)S(1)} %fusion.16), custom_call_target="Cholesky" | custom-call | tf_op jit(solution)/shard_map/jit(cholesky)/cholesky | solution.py:33
  372.7 1.3 select_bitcast_fusion.4
  373.9 10.6 %custom-call.17 = f32[1,128,128]{1,2,0:T(8,128)S(1)} custom-call(f32[1,128,128]{2,1,0:T(8,128)} %get-tuple-element.131), custom_call_target="InvertDiagBlocksLowerTriangular" | custom-call | tf_op jit(solution)/shard_map/triangular_solve/custom-call.0 | solution.py:34
  384.6 1.4 copy.57
  386.0 2.3 fusion.4
  391.5 19.5 %all_to_all.47 = f32[16,128,128]{1,2,0:T(8,128)S(1)} all-to-all(f32[16,128,128]{1,2,0:T(8,128)S(1)} %stack.23), channel_id=1, replica_groups=mesh['sub'=16,'fr'=16] {'fr'}, dimensions={0} | all-to-all | bytes 2097152 | tf_op jit(solution)/shard_map/all_to_all | solution.py:24
  411.2 11.7 %cholesky.204 = f32[128,128]{1,0:T(8,128)S(1)} custom-call(f32[128,128]{1,0:T(8,128)S(1)} %fusion.15), custom_call_target="Cholesky" | custom-call | tf_op jit(solution)/shard_map/jit(cholesky)/cholesky | solution.py:33
  424.2 10.4 %custom-call.18 = f32[1,128,128]{1,2,0:T(8,128)} custom-call(f32[1,128,128]{2,1,0:T(8,128)S(1)} %get-tuple-element.129), custom_call_target="InvertDiagBlocksLowerTriangular" | custom-call | tf_op jit(solution)/shard_map/triangular_solve/custom-call.0 | solution.py:34
  435.0 1.9 fusion.3
  438.0 3.3 convolution_subtract_fusion.2
  445.1 110.9 %all-gather.5.cloned.1.call-done = f32[2048,2048]{1,0:T(8,128)} async-done(((f32[128,2048]{1,0:T(8,128)}), f32[2048,2048]{1,0:T(8,128)}) %all-gather.5.cloned.1.call-update) | async-done | bytes 16777232 | tf_op jit(solution)/shard_map/all_gather | solution.py:64
  556.0 7.2 gather_fusion.1
  564.6 1.8 collective-permute-start.2
  566.4 23.2 %collective-permute-done.2 = f32[128,2048]{1,0:T(8,128)S(1)} collective-permute-done((f32[128,2048]{1,0:T(8,128)S(1)}, f32[128,2048]{1,0:T(8,128)S(1)}, u32[]{:S(2)}, u32[]{:S(2)}) %collective-permute-start.2) | collective-permute-done | bytes 1048608 | tf_op jit(solution)/shard_map/ppermute | solution.py:14
  590.0 20.4 %all_to_all.48 = f32[16,128,128]{1,2,0:T(8,128)S(1)} all-to-all(f32[16,128,128]{1,2,0:T(8,128)S(1)} %stack.24), channel_id=1, replica_groups=mesh['sub'=16,'fr'=16] {'fr'}, dimensions={0} | all-to-all | bytes 2097152 | tf_op jit(solution)/shard_map/all_to_all | solution.py:24
  611.0 1.6 copy.64
  612.5 1.5 fusion.14
  614.0 13.2 %cholesky.215 = f32[128,128]{1,0:T(8,128)} custom-call(f32[128,128]{1,0:T(8,128)} %fusion.14), custom_call_target="Cholesky" | custom-call | tf_op jit(solution)/shard_map/jit(cholesky)/cholesky | solution.py:33
  628.7 2.2 select_bitcast_fusion.2
  630.9 11.3 %custom-call.19 = f32[1,128,128]{1,2,0:T(8,128)} custom-call(f32[1,128,128]{2,1,0:T(8,128)} %get-tuple-element.127), custom_call_target="InvertDiagBlocksLowerTriangular" | custom-call | tf_op jit(solution)/shard_map/triangular_solve/custom-call.0 | solution.py:34
  642.2 1.3 copy.65
  643.5 2.3 fusion.2
  649.1 5.2 all-to-all-start.7
  661.4 1.5 constant_dynamic-slice_fusion.6
  662.9 5.7 all-to-all-done.7
  668.7 11.7 %cholesky.226 = f32[128,128]{1,0:T(8,128)S(1)} custom-call(f32[128,128]{1,0:T(8,128)S(1)} %fusion.13), custom_call_target="Cholesky" | custom-call | tf_op jit(solution)/shard_map/jit(cholesky)/cholesky | solution.py:33
  681.8 9.8 %custom-call.20 = f32[1,128,128]{1,2,0:T(8,128)S(1)} custom-call(f32[1,128,128]{2,1,0:T(8,128)S(1)} %get-tuple-element.125), custom_call_target="InvertDiagBlocksLowerTriangular" | custom-call | tf_op jit(solution)/shard_map/triangular_solve/custom-call.0 | solution.py:34
  693.0 2.3 convolution_subtract_fusion
  695.5 1.2 stack.26
  696.7 5.2 all-to-all-start.8
  707.8 7.6 %all-to-all-done.8 = f32[16,128,128]{1,2,0:T(8,128)S(1)} async-done(((f32[16,128,128]{1,2,0:T(8,128)}), f32[16,128,128]{1,2,0:T(8,128)S(1)}, u32[]{:S(2)}, u32[]{:S(2)}) %all-to-all-start.8) | async-done | bytes 1048608 | tf_op jit(solution)/shard_map/all_to_all | solution.py:24
  715.6 11.7 %cholesky.237 = f32[128,128]{1,0:T(8,128)S(1)} custom-call(f32[128,128]{1,0:T(8,128)S(1)} %fusion.12), custom_call_target="Cholesky" | custom-call | tf_op jit(solution)/shard_map/jit(cholesky)/cholesky | solution.py:33
  728.6 9.8 %custom-call.21 = f32[1,128,128]{1,2,0:T(8,128)S(1)} custom-call(f32[1,128,128]{2,1,0:T(8,128)S(1)} %get-tuple-element.123), custom_call_target="InvertDiagBlocksLowerTriangular" | custom-call | tf_op jit(solution)/shard_map/triangular_solve/custom-call.0 | solution.py:34
  741.9 2.3 fusion.11
  (171 shorter events, 56.1 us)
Async XLA Ops:
  7.2 434.2 %copy-start = (s32[8,13]{1,0:T(8,128)S(1)}, s32[8,13]{1,0:T(8,128)}, u32[]{:S(2)}) copy-start(s32[8,13]{1,0:T(8,128)} %param.32) | copy-start | bytes 1252
  9.1 23.3 %all-to-all-start = ((f32[16,128,128]{1,2,0:T(8,128)}), f32[16,128,128]{1,2,0:T(8,128)S(1)}, u32[]{:S(2)}, u32[]{:S(2)}) async-start(f32[16,128,128]{1,2,0:T(8,128)} %stack.18), calls=%async_computation | async-start | bytes 2097152 | tf_op jit(solution)/shard_map/all_to_all | solution.py:24
  59.0 1.0 copy-start.7
  61.2 20.7 %all-to-all-start.1 = ((f32[16,128,128]{1,2,0:T(8,128)}), f32[16,128,128]{1,2,0:T(8,128)S(1)}, u32[]{:S(2)}, u32[]{:S(2)}) async-start(f32[16,128,128]{1,2,0:T(8,128)} %stack.19), calls=%async_computation.1 | async-start | bytes 2097152 | tf_op jit(solution)/shard_map/all_to_all | solution.py:24
  106.4 1.0 copy-start.1
  110.9 20.0 %all-to-all-start.2 = ((f32[16,128,128]{1,2,0:T(8,128)}), f32[16,128,128]{1,2,0:T(8,128)S(1)}, u32[]{:S(2)}, u32[]{:S(2)}) async-start(f32[16,128,128]{1,2,0:T(8,128)} %stack.20), calls=%async_computation.2 | async-start | bytes 2097152 | tf_op jit(solution)/shard_map/all_to_all | solution.py:24
  115.7 163.3 %all-gather.3.cloned.1.call-start = ((), (), s32[]{:S(2)}) async-start(), calls=%async_computation.9 | async-start | bytes 17825792 | tf_op jit(solution)/shard_map/all_gather | solution.py:64
  144.7 142.6 %copy-start.10 = (f32[128,384]{1,0:T(8,128)S(1)}, f32[128,384]{1,0:T(8,128)}, u32[]{:S(2)}) copy-start(f32[128,384]{1,0:T(8,128)} %param.29) | copy-start | bytes 589828
  159.6 1.0 copy-start.2
  162.7 393.3 %all-gather.5.cloned.1.call-start = ((), (), s32[]{:S(2)}) async-start(), calls=%async_computation.10 | async-start | bytes 17825792 | tf_op jit(solution)/shard_map/all_gather | solution.py:64
  287.7 2.7 collective-permute-start
  339.0 1.1 copy-start.4
  388.3 1.0 copy-start.3
  390.3 1.0 copy-start.8
  436.9 1.0 copy-start.5
  441.3 2.9 collective-permute-start.1
  564.6 25.0 %collective-permute-start.2 = (f32[128,2048]{1,0:T(8,128)S(1)}, f32[128,2048]{1,0:T(8,128)S(1)}, u32[]{:S(2)}, u32[]{:S(2)}) collective-permute-start(f32[128,2048]{1,0:T(8,128)S(1)} %bitcast_add_fusion), channel_id=1, source_target_pairs={{0,32},{16,48},{32,0},{48,16},{64,96},{80,112},{96,64},{112,80},{1... | collective-permute-start | bytes 3145736 | tf_op jit(solution)/shard_map/ppermute | solution.py:14
  646.9 1.0 copy-start.6
  649.1 19.5 %all-to-all-start.7 = ((f32[16,128,128]{1,2,0:T(8,128)}), f32[16,128,128]{1,2,0:T(8,128)S(1)}, u32[]{:S(2)}, u32[]{:S(2)}) async-start(f32[16,128,128]{1,2,0:T(8,128)} %stack.25), calls=%async_computation.7 | async-start | bytes 2097152 | tf_op jit(solution)/shard_map/all_to_all | solution.py:24
  695.3 1.4 copy-start.9
  696.7 18.8 %all-to-all-start.8 = ((f32[16,128,128]{1,2,0:T(8,128)}), f32[16,128,128]{1,2,0:T(8,128)S(1)}, u32[]{:S(2)}, u32[]{:S(2)}) async-start(f32[16,128,128]{1,2,0:T(8,128)} %stack.26), calls=%async_computation.8 | async-start | bytes 2097152 | tf_op jit(solution)/shard_map/all_to_all | solution.py:24
Sparse Core Ops, SparseCore 0:
  162.9 116.1 all-gather.2
  441.4 114.5 all-gather.4
